TPU v7x, 128 devices: a whole 4x4x4 slice. The times are simulated.
128 devices in a mesh: tm: 32 (over x, z, core), chan: 4 (over y).
Axes of the slice: x: 4, y: 4, z: 4, core: 2. Of those that a mesh axis runs over, the one named last changes fastest.
Arguments:
- inputs: bfloat16 [64, 256, 512], P('tm'), may hold values from -6 to 6
- decay: float32 [64, 512], P('tm', 'chan'), may hold values from 0 to 1, as said below
- kernel_b: bfloat16 [9, 512, 256], P(None, 'chan'), may hold values from -0.125 to 0.125
- kernel_c: bfloat16 [9, 256, 512], P(None, 'chan'), may hold values from -0.09375 to 0.09375
- cotangent: bfloat16 [64, 256, 512], P('tm', 'chan'), may hold values from -0.03125 to 0.03125
Outputs:
- grad_b: float32 [9, 512, 256], P(None, 'chan')
- grad_c: float32 [9, 256, 512], P(None, 'chan')
- decay_grad: float32 [64, 512], P('tm', 'chan')
Inputs may be any that keep to these rules, and one draw needn't show every extreme that they name: decay lies strictly between 0 and 1.
All inputs are finite; a program needn't handle non-finite values.
Results may differ from a plain program's by a relative error of at most 0.003.
Values may be sent and summed in bfloat16 or wider, within the bound.
No kernel may reach another device: no remote copies, remote signals or barrier semaphores. Data moves between devices by JAX's collectives and lax.ppermute only.
A program may use at most 128 MiB of HBM per device.

v0:
```python
import jax
import jax.numpy as jnp
from jax import lax
from jax.sharding import PartitionSpec as P

W = 64
offsets = ((-1, -1), (-1, 0), (-1, 1), (0, -1), (0, 0), (0, 1), (1, -1), (1, 0), (1, 1))


def passed_along(value, axis, steps):
    count = lax.axis_size(axis)
    first, last = (max(0, -steps), min(count, count - steps))
    return lax.ppermute(value, axis, [(source, source + steps) for source in range(first, last)])


def shift_cells(source, row_shift, col_shift, grid_width):
    cell_count = source.shape[-1]
    margin = grid_width + 1
    padded = jnp.pad(source, [(0, 0)] * (source.ndim - 1) + [(margin, margin)])
    first_cell = margin + row_shift * grid_width + col_shift
    shifted = lax.slice_in_dim(padded, first_cell, first_cell + cell_count, axis=source.ndim - 1)
    column = jnp.arange(cell_count) % grid_width
    inside = (column + col_shift >= 0) & (column + col_shift < grid_width)
    return jnp.where(inside, shifted, jnp.zeros((), source.dtype))


def stencil_stack(source, grid_width, decay_factor):
    parts = [
        shift_cells(source, decay_factor * pair[0], decay_factor * pair[1], grid_width)
        for pair in offsets
    ]
    return jnp.stack(parts, axis=source.ndim - 2)


def body(inputs, decay, kernel_b, kernel_c, cotangent):
    local_rows = kernel_b.shape[1]
    cell_count = inputs.shape[-1]
    blank_state = jnp.zeros((local_rows, cell_count), jnp.float32)
    input_stack = stencil_stack(inputs, W, 1)
    drives = jnp.einsum("kpc,fkcs->fps", kernel_b, input_stack, preferred_element_type=jnp.float32)

    def advance(current, frame_pair):
        frame_rate, drive = frame_pair
        current = frame_rate[:, None] * current + drive
        return (current, current)

    local_end, local_states = lax.scan(advance, blank_state, (decay, drives))
    decay_total = jnp.prod(decay, axis=0)

    def relay_state(turn_index, carried):
        outgoing = decay_total[:, None] * carried + local_end
        return passed_along(outgoing, "tm", 1)

    entering = lax.fori_loop(0, lax.axis_size("tm") - 1, relay_state, blank_state)
    cumulative = jnp.cumprod(decay, axis=0)
    states = local_states + cumulative[:, :, None] * entering[None]
    previous = jnp.concatenate([entering[None], states[:-1]], axis=0)
    states_bf = states.astype(jnp.bfloat16)
    cot_stack = stencil_stack(cotangent, W, -1)
    injected = lax.psum_scatter(
        jnp.einsum("kup,fkus->pfs", kernel_c, cot_stack, preferred_element_type=jnp.float32),
        "chan",
        scatter_dimension=0,
        tiled=True,
    )
    injected = jnp.moveaxis(injected, 1, 0)

    def retreat(carried, frame_pair):
        frame_rate, source = frame_pair
        adjoint = source + carried
        return (frame_rate[:, None] * adjoint, adjoint)

    message, local_adjoint = lax.scan(retreat, blank_state, (decay, injected), reverse=True)

    def relay_adjoint(turn_index, carried):
        outgoing = decay_total[:, None] * carried + message
        return passed_along(outgoing, "tm", -1)

    arriving = lax.fori_loop(0, lax.axis_size("tm") - 1, relay_adjoint, blank_state)
    suffix = jnp.flip(jnp.cumprod(jnp.flip(decay, 0), 0), 0)
    later_decay = jnp.concatenate([suffix[1:], jnp.ones_like(decay[:1])], axis=0)
    adjoint = local_adjoint + later_decay[:, :, None] * arriving[None]
    decay_grad = jnp.sum(adjoint * previous, axis=2)
    adjoint_bf = adjoint.astype(jnp.bfloat16)
    grad_b_part = jnp.einsum(
        "fps,fkcs->kpc", adjoint_bf, input_stack, preferred_element_type=jnp.float32
    )
    shifted = stencil_stack(lax.all_gather(states_bf, "chan", axis=1, tiled=True), W, 1)
    grad_c_part = jnp.einsum(
        "fus,fkps->kup", cotangent, shifted, preferred_element_type=jnp.float32
    )
    grad_b, grad_c = lax.psum((grad_b_part, grad_c_part), "tm")
    return (grad_b, grad_c, decay_grad)


def solution(mesh):
    in_specs = (
        P("tm", None, None),
        P("tm", "chan"),
        P(None, "chan", None),
        P(None, "chan", None),
        P("tm", "chan", None),
    )
    out_specs = (P(None, "chan", None), P(None, "chan", None), P("tm", "chan"))
    return jax.shard_map(body, mesh=mesh, in_specs=in_specs, out_specs=out_specs, check_vma=False)
```

profile of v0, /device:TPU:1, one launch (start us, length us, event | category | flops | bytes accessed | tf_op | source)
XLA Modules:
  0.0 817.5 jit_solution(8985757919530302460)
XLA Ops:
  20.7 275.2 %while.51 = (s32[]{:T(128)}, f32[128,512]{1,0:T(8,128)S(1)}, f32[128]{0:T(128)S(1)}, f32[128,512]{1,0:T(8,128)S(1)}, s32[]{:T(128)}) while((s32[]{:T(128)}, f32[128,512]{1,0:T(8,128)S(1)}, f32[128]{0:T(128)S(1)}, f32[128,512]{1,0:T(8,128)S(1)}, s32[]{:T(128)}) %tuple.101), condition=%wide.region_12.13_spmd, body=%wide.region_11.12_spmd.sunk | while | flops 131074 | bytes 1835621 | solution.py:54
  138.1 6.0 collective-permute-start.1
  147.5 6.5 collective-permute-start.1
  157.4 6.5 collective-permute-start.1
  167.3 6.5 collective-permute-start.1
  177.2 6.5 collective-permute-start.1
  187.1 6.5 collective-permute-start.1
  197.0 6.5 collective-permute-start.1
  206.9 6.5 collective-permute-start.1
  216.8 6.5 collective-permute-start.1
  226.7 6.5 collective-permute-start.1
  236.6 6.5 collective-permute-start.1
  246.5 6.5 collective-permute-start.1
  256.4 6.5 collective-permute-start.1
  266.3 6.5 collective-permute-start.1
  276.2 6.5 collective-permute-start.1
  286.1 6.5 collective-permute-start.1
  300.5 49.7 %all-gather.2.cloned.1.call-done = bf16[2,512,512]{2,1,0:T(8,128)(2,1)} async-done(((bf16[2,128,512]{2,1,0:T(8,128)(2,1)}), bf16[2,512,512]{2,1,0:T(8,128)(2,1)}) %all-gather.2.cloned.1.call-update) | async-done | bytes 1048592 | tf_op jit(solution)/shard_map/all_gather | solution.py:88
  361.1 23.6 %reduce-scatter.2.cloned.1.call-done = f32[128,2,512]{0,2,1:T(8,128)} async-done(((f32[512,2,512]{0,2,1:T(8,128)}), f32[128,2,512]{0,2,1:T(8,128)}) %reduce-scatter.2.cloned.1.call-update) | async-done | bytes 524304 | tf_op jit(solution)/shard_map/reduce_scatter | solution.py:60
  387.4 279.4 %while.50 = (s32[]{:T(128)}, f32[128,512]{1,0:T(8,128)S(1)}, f32[128]{0:T(128)S(1)}, f32[128,512]{1,0:T(8,128)S(1)}, s32[]{:T(128)}) while((s32[]{:T(128)}, f32[128,512]{1,0:T(8,128)S(1)}, f32[128]{0:T(128)S(1)}, f32[128,512]{1,0:T(8,128)S(1)}, s32[]{:T(128)}) %tuple.113), condition=%wide.region_6.7_spmd, body=%wide.region_5.6_spmd.sunk | while | flops 131074 | bytes 1835621 | solution.py:79
  397.4 5.8 collective-permute-done
  405.2 5.8 collective-permute-done
  413.0 5.8 collective-permute-done
  420.8 5.8 collective-permute-done
  428.5 5.8 collective-permute-done
  436.3 5.8 collective-permute-done
  444.1 5.8 collective-permute-done
  451.9 5.8 collective-permute-done
  483.0 5.8 collective-permute-done
  490.8 7.7 collective-permute-done
  500.6 7.9 collective-permute-done
  510.5 7.9 collective-permute-done
  520.4 7.9 collective-permute-done
  530.3 7.9 collective-permute-done
  540.2 7.9 collective-permute-done
  550.0 7.9 collective-permute-done
  559.9 7.9 collective-permute-done
  569.8 7.9 collective-permute-done
  579.7 7.9 collective-permute-done
  589.6 7.9 collective-permute-done
  599.5 7.9 collective-permute-done
  609.4 7.9 collective-permute-done
  619.3 7.9 collective-permute-done
  629.2 7.9 collective-permute-done
  639.1 7.9 collective-permute-done
  649.0 7.9 collective-permute-done
  658.9 7.9 collective-permute-done
  672.4 133.6 %all-reduce.6.cloned.1.call-done = (f32[9,128,256]{1,2,0:T(8,128)}, f32[9,64,512]{2,1,0:T(8,128)}) async-done(((f32[9,128,256]{1,2,0:T(8,128)}, f32[9,64,512]{2,1,0:T(8,128)}), (f32[9,128,256]{1,2,0:T(8,128)}, f32[9,64,512]{2,1,0:T(8,128)})) %all-reduce.6.cloned.1.call-update) | async-done | bytes 2359312 | tf_op jit(solution)/shard_map/psum | solution.py:92
  (235 shorter events, 301.6 us)
Async XLA Ops:
  7.2 343.0 %all-gather.2.cloned.1.call-start = ((), (), s32[]{:S(2)}) async-start(), calls=%async_computation.2 | async-start | bytes 1310720 | tf_op jit(solution)/shard_map/all_gather | solution.py:88
  20.8 8.2 %collective-permute-start.1 = (f32[128,512]{1,0:T(8,128)S(1)}, f32[128,512]{1,0:T(8,128)S(1)}, u32[]{:S(2)}, u32[]{:S(2)}) collective-permute-start(f32[128,512]{1,0:T(8,128)S(1)} %multiply_add_fusion.8), channel_id=1, source_target_pairs={{0,4},{4,8},{8,12},{12,16},{16,20},{20,24},{24,28},{28,32},{32,36}... | collective-permute-start | bytes 786440 | tf_op jit(solution)/shard_map/while/body/eval_jaxpr/ppermute | solution.py:13
  29.1 7.7 collective-permute-start.1
  36.9 7.7 collective-permute-start.1
  44.7 7.7 collective-permute-start.1
  60.2 7.7 collective-permute-start.1
  68.0 7.7 collective-permute-start.1
  75.8 7.7 collective-permute-start.1
  83.6 7.7 collective-permute-start.1
  91.4 7.7 collective-permute-start.1
  99.2 7.7 collective-permute-start.1
  138.1 9.3 %collective-permute-start.1 = (f32[128,512]{1,0:T(8,128)S(1)}, f32[128,512]{1,0:T(8,128)S(1)}, u32[]{:S(2)}, u32[]{:S(2)}) collective-permute-start(f32[128,512]{1,0:T(8,128)S(1)} %multiply_add_fusion.8), channel_id=1, source_target_pairs={{0,4},{4,8},{8,12},{12,16},{16,20},{20,24},{24,28},{28,32},{32,36}... | collective-permute-start | bytes 786440 | tf_op jit(solution)/shard_map/while/body/eval_jaxpr/ppermute | solution.py:13
  147.5 9.8 %collective-permute-start.1 = (f32[128,512]{1,0:T(8,128)S(1)}, f32[128,512]{1,0:T(8,128)S(1)}, u32[]{:S(2)}, u32[]{:S(2)}) collective-permute-start(f32[128,512]{1,0:T(8,128)S(1)} %multiply_add_fusion.8), channel_id=1, source_target_pairs={{0,4},{4,8},{8,12},{12,16},{16,20},{20,24},{24,28},{28,32},{32,36}... | collective-permute-start | bytes 786440 | tf_op jit(solution)/shard_map/while/body/eval_jaxpr/ppermute | solution.py:13
  157.4 9.8 %collective-permute-start.1 = (f32[128,512]{1,0:T(8,128)S(1)}, f32[128,512]{1,0:T(8,128)S(1)}, u32[]{:S(2)}, u32[]{:S(2)}) collective-permute-start(f32[128,512]{1,0:T(8,128)S(1)} %multiply_add_fusion.8), channel_id=1, source_target_pairs={{0,4},{4,8},{8,12},{12,16},{16,20},{20,24},{24,28},{28,32},{32,36}... | collective-permute-start | bytes 786440 | tf_op jit(solution)/shard_map/while/body/eval_jaxpr/ppermute | solution.py:13
  167.3 9.8 %collective-permute-start.1 = (f32[128,512]{1,0:T(8,128)S(1)}, f32[128,512]{1,0:T(8,128)S(1)}, u32[]{:S(2)}, u32[]{:S(2)}) collective-permute-start(f32[128,512]{1,0:T(8,128)S(1)} %multiply_add_fusion.8), channel_id=1, source_target_pairs={{0,4},{4,8},{8,12},{12,16},{16,20},{20,24},{24,28},{28,32},{32,36}... | collective-permute-start | bytes 786440 | tf_op jit(solution)/shard_map/while/body/eval_jaxpr/ppermute | solution.py:13
  177.2 9.8 %collective-permute-start.1 = (f32[128,512]{1,0:T(8,128)S(1)}, f32[128,512]{1,0:T(8,128)S(1)}, u32[]{:S(2)}, u32[]{:S(2)}) collective-permute-start(f32[128,512]{1,0:T(8,128)S(1)} %multiply_add_fusion.8), channel_id=1, source_target_pairs={{0,4},{4,8},{8,12},{12,16},{16,20},{20,24},{24,28},{28,32},{32,36}... | collective-permute-start | bytes 786440 | tf_op jit(solution)/shard_map/while/body/eval_jaxpr/ppermute | solution.py:13
  187.1 9.8 %collective-permute-start.1 = (f32[128,512]{1,0:T(8,128)S(1)}, f32[128,512]{1,0:T(8,128)S(1)}, u32[]{:S(2)}, u32[]{:S(2)}) collective-permute-start(f32[128,512]{1,0:T(8,128)S(1)} %multiply_add_fusion.8), channel_id=1, source_target_pairs={{0,4},{4,8},{8,12},{12,16},{16,20},{20,24},{24,28},{28,32},{32,36}... | collective-permute-start | bytes 786440 | tf_op jit(solution)/shard_map/while/body/eval_jaxpr/ppermute | solution.py:13
  197.0 9.8 %collective-permute-start.1 = (f32[128,512]{1,0:T(8,128)S(1)}, f32[128,512]{1,0:T(8,128)S(1)}, u32[]{:S(2)}, u32[]{:S(2)}) collective-permute-start(f32[128,512]{1,0:T(8,128)S(1)} %multiply_add_fusion.8), channel_id=1, source_target_pairs={{0,4},{4,8},{8,12},{12,16},{16,20},{20,24},{24,28},{28,32},{32,36}... | collective-permute-start | bytes 786440 | tf_op jit(solution)/shard_map/while/body/eval_jaxpr/ppermute | solution.py:13
  206.9 9.8 %collective-permute-start.1 = (f32[128,512]{1,0:T(8,128)S(1)}, f32[128,512]{1,0:T(8,128)S(1)}, u32[]{:S(2)}, u32[]{:S(2)}) collective-permute-start(f32[128,512]{1,0:T(8,128)S(1)} %multiply_add_fusion.8), channel_id=1, source_target_pairs={{0,4},{4,8},{8,12},{12,16},{16,20},{20,24},{24,28},{28,32},{32,36}... | collective-permute-start | bytes 786440 | tf_op jit(solution)/shard_map/while/body/eval_jaxpr/ppermute | solution.py:13
  216.8 9.8 %collective-permute-start.1 = (f32[128,512]{1,0:T(8,128)S(1)}, f32[128,512]{1,0:T(8,128)S(1)}, u32[]{:S(2)}, u32[]{:S(2)}) collective-permute-start(f32[128,512]{1,0:T(8,128)S(1)} %multiply_add_fusion.8), channel_id=1, source_target_pairs={{0,4},{4,8},{8,12},{12,16},{16,20},{20,24},{24,28},{28,32},{32,36}... | collective-permute-start | bytes 786440 | tf_op jit(solution)/shard_map/while/body/eval_jaxpr/ppermute | solution.py:13
  226.7 9.8 %collective-permute-start.1 = (f32[128,512]{1,0:T(8,128)S(1)}, f32[128,512]{1,0:T(8,128)S(1)}, u32[]{:S(2)}, u32[]{:S(2)}) collective-permute-start(f32[128,512]{1,0:T(8,128)S(1)} %multiply_add_fusion.8), channel_id=1, source_target_pairs={{0,4},{4,8},{8,12},{12,16},{16,20},{20,24},{24,28},{28,32},{32,36}... | collective-permute-start | bytes 786440 | tf_op jit(solution)/shard_map/while/body/eval_jaxpr/ppermute | solution.py:13
  236.6 9.8 %collective-permute-start.1 = (f32[128,512]{1,0:T(8,128)S(1)}, f32[128,512]{1,0:T(8,128)S(1)}, u32[]{:S(2)}, u32[]{:S(2)}) collective-permute-start(f32[128,512]{1,0:T(8,128)S(1)} %multiply_add_fusion.8), channel_id=1, source_target_pairs={{0,4},{4,8},{8,12},{12,16},{16,20},{20,24},{24,28},{28,32},{32,36}... | collective-permute-start | bytes 786440 | tf_op jit(solution)/shard_map/while/body/eval_jaxpr/ppermute | solution.py:13
  246.5 9.8 %collective-permute-start.1 = (f32[128,512]{1,0:T(8,128)S(1)}, f32[128,512]{1,0:T(8,128)S(1)}, u32[]{:S(2)}, u32[]{:S(2)}) collective-permute-start(f32[128,512]{1,0:T(8,128)S(1)} %multiply_add_fusion.8), channel_id=1, source_target_pairs={{0,4},{4,8},{8,12},{12,16},{16,20},{20,24},{24,28},{28,32},{32,36}... | collective-permute-start | bytes 786440 | tf_op jit(solution)/shard_map/while/body/eval_jaxpr/ppermute | solution.py:13
  256.4 9.8 %collective-permute-start.1 = (f32[128,512]{1,0:T(8,128)S(1)}, f32[128,512]{1,0:T(8,128)S(1)}, u32[]{:S(2)}, u32[]{:S(2)}) collective-permute-start(f32[128,512]{1,0:T(8,128)S(1)} %multiply_add_fusion.8), channel_id=1, source_target_pairs={{0,4},{4,8},{8,12},{12,16},{16,20},{20,24},{24,28},{28,32},{32,36}... | collective-permute-start | bytes 786440 | tf_op jit(solution)/shard_map/while/body/eval_jaxpr/ppermute | solution.py:13
  266.3 9.8 %collective-permute-start.1 = (f32[128,512]{1,0:T(8,128)S(1)}, f32[128,512]{1,0:T(8,128)S(1)}, u32[]{:S(2)}, u32[]{:S(2)}) collective-permute-start(f32[128,512]{1,0:T(8,128)S(1)} %multiply_add_fusion.8), channel_id=1, source_target_pairs={{0,4},{4,8},{8,12},{12,16},{16,20},{20,24},{24,28},{28,32},{32,36}... | collective-permute-start | bytes 786440 | tf_op jit(solution)/shard_map/while/body/eval_jaxpr/ppermute | solution.py:13
  276.2 9.8 %collective-permute-start.1 = (f32[128,512]{1,0:T(8,128)S(1)}, f32[128,512]{1,0:T(8,128)S(1)}, u32[]{:S(2)}, u32[]{:S(2)}) collective-permute-start(f32[128,512]{1,0:T(8,128)S(1)} %multiply_add_fusion.8), channel_id=1, source_target_pairs={{0,4},{4,8},{8,12},{12,16},{16,20},{20,24},{24,28},{28,32},{32,36}... | collective-permute-start | bytes 786440 | tf_op jit(solution)/shard_map/while/body/eval_jaxpr/ppermute | solution.py:13
  286.1 9.8 %collective-permute-start.1 = (f32[128,512]{1,0:T(8,128)S(1)}, f32[128,512]{1,0:T(8,128)S(1)}, u32[]{:S(2)}, u32[]{:S(2)}) collective-permute-start(f32[128,512]{1,0:T(8,128)S(1)} %multiply_add_fusion.8), channel_id=1, source_target_pairs={{0,4},{4,8},{8,12},{12,16},{16,20},{20,24},{24,28},{28,32},{32,36}... | collective-permute-start | bytes 786440 | tf_op jit(solution)/shard_map/while/body/eval_jaxpr/ppermute | solution.py:13
  296.7 88.0 %reduce-scatter.2.cloned.1.call-start = ((), (), s32[]{:S(2)}) async-start(), calls=%async_computation.1 | async-start | bytes 2621440 | tf_op jit(solution)/shard_map/reduce_scatter | solution.py:60
  300.2 505.8 %all-reduce.6.cloned.1.call-start = ((), (), s32[]{:S(2)}) async-start(), calls=%async_computation.3 | async-start | bytes 4718592 | tf_op jit(solution)/shard_map/psum | solution.py:92
  387.5 7.9 collective-permute-start
  488.9 9.6 %collective-permute-start = (f32[128,512]{1,0:T(8,128)S(1)}, f32[128,512]{1,0:T(8,128)S(1)}, u32[]{:S(2)}, u32[]{:S(2)}) collective-permute-start(f32[128,512]{1,0:T(8,128)S(1)} %multiply_add_fusion.7), channel_id=1, source_target_pairs={{4,0},{8,4},{12,8},{16,12},{20,16},{24,20},{28,24},{32,28},{36,32}... | collective-permute-start | bytes 786440 | tf_op jit(solution)/shard_map/while/body/eval_jaxpr/ppermute | solution.py:13
  498.6 9.8 %collective-permute-start = (f32[128,512]{1,0:T(8,128)S(1)}, f32[128,512]{1,0:T(8,128)S(1)}, u32[]{:S(2)}, u32[]{:S(2)}) collective-permute-start(f32[128,512]{1,0:T(8,128)S(1)} %multiply_add_fusion.7), channel_id=1, source_target_pairs={{4,0},{8,4},{12,8},{16,12},{20,16},{24,20},{28,24},{32,28},{36,32}... | collective-permute-start | bytes 786440 | tf_op jit(solution)/shard_map/while/body/eval_jaxpr/ppermute | solution.py:13
  508.5 9.8 %collective-permute-start = (f32[128,512]{1,0:T(8,128)S(1)}, f32[128,512]{1,0:T(8,128)S(1)}, u32[]{:S(2)}, u32[]{:S(2)}) collective-permute-start(f32[128,512]{1,0:T(8,128)S(1)} %multiply_add_fusion.7), channel_id=1, source_target_pairs={{4,0},{8,4},{12,8},{16,12},{20,16},{24,20},{28,24},{32,28},{36,32}... | collective-permute-start | bytes 786440 | tf_op jit(solution)/shard_map/while/body/eval_jaxpr/ppermute | solution.py:13
  518.4 9.8 %collective-permute-start = (f32[128,512]{1,0:T(8,128)S(1)}, f32[128,512]{1,0:T(8,128)S(1)}, u32[]{:S(2)}, u32[]{:S(2)}) collective-permute-start(f32[128,512]{1,0:T(8,128)S(1)} %multiply_add_fusion.7), channel_id=1, source_target_pairs={{4,0},{8,4},{12,8},{16,12},{20,16},{24,20},{28,24},{32,28},{36,32}... | collective-permute-start | bytes 786440 | tf_op jit(solution)/shard_map/while/body/eval_jaxpr/ppermute | solution.py:13
  528.3 9.8 %collective-permute-start = (f32[128,512]{1,0:T(8,128)S(1)}, f32[128,512]{1,0:T(8,128)S(1)}, u32[]{:S(2)}, u32[]{:S(2)}) collective-permute-start(f32[128,512]{1,0:T(8,128)S(1)} %multiply_add_fusion.7), channel_id=1, source_target_pairs={{4,0},{8,4},{12,8},{16,12},{20,16},{24,20},{28,24},{32,28},{36,32}... | collective-permute-start | bytes 786440 | tf_op jit(solution)/shard_map/while/body/eval_jaxpr/ppermute | solution.py:13
  538.2 9.8 %collective-permute-start = (f32[128,512]{1,0:T(8,128)S(1)}, f32[128,512]{1,0:T(8,128)S(1)}, u32[]{:S(2)}, u32[]{:S(2)}) collective-permute-start(f32[128,512]{1,0:T(8,128)S(1)} %multiply_add_fusion.7), channel_id=1, source_target_pairs={{4,0},{8,4},{12,8},{16,12},{20,16},{24,20},{28,24},{32,28},{36,32}... | collective-permute-start | bytes 786440 | tf_op jit(solution)/shard_map/while/body/eval_jaxpr/ppermute | solution.py:13
  548.1 9.8 %collective-permute-start = (f32[128,512]{1,0:T(8,128)S(1)}, f32[128,512]{1,0:T(8,128)S(1)}, u32[]{:S(2)}, u32[]{:S(2)}) collective-permute-start(f32[128,512]{1,0:T(8,128)S(1)} %multiply_add_fusion.7), channel_id=1, source_target_pairs={{4,0},{8,4},{12,8},{16,12},{20,16},{24,20},{28,24},{32,28},{36,32}... | collective-permute-start | bytes 786440 | tf_op jit(solution)/shard_map/while/body/eval_jaxpr/ppermute | solution.py:13
  558.0 9.8 %collective-permute-start = (f32[128,512]{1,0:T(8,128)S(1)}, f32[128,512]{1,0:T(8,128)S(1)}, u32[]{:S(2)}, u32[]{:S(2)}) collective-permute-start(f32[128,512]{1,0:T(8,128)S(1)} %multiply_add_fusion.7), channel_id=1, source_target_pairs={{4,0},{8,4},{12,8},{16,12},{20,16},{24,20},{28,24},{32,28},{36,32}... | collective-permute-start | bytes 786440 | tf_op jit(solution)/shard_map/while/body/eval_jaxpr/ppermute | solution.py:13
  567.9 9.8 %collective-permute-start = (f32[128,512]{1,0:T(8,128)S(1)}, f32[128,512]{1,0:T(8,128)S(1)}, u32[]{:S(2)}, u32[]{:S(2)}) collective-permute-start(f32[128,512]{1,0:T(8,128)S(1)} %multiply_add_fusion.7), channel_id=1, source_target_pairs={{4,0},{8,4},{12,8},{16,12},{20,16},{24,20},{28,24},{32,28},{36,32}... | collective-permute-start | bytes 786440 | tf_op jit(solution)/shard_map/while/body/eval_jaxpr/ppermute | solution.py:13
  577.8 9.8 %collective-permute-start = (f32[128,512]{1,0:T(8,128)S(1)}, f32[128,512]{1,0:T(8,128)S(1)}, u32[]{:S(2)}, u32[]{:S(2)}) collective-permute-start(f32[128,512]{1,0:T(8,128)S(1)} %multiply_add_fusion.7), channel_id=1, source_target_pairs={{4,0},{8,4},{12,8},{16,12},{20,16},{24,20},{28,24},{32,28},{36,32}... | collective-permute-start | bytes 786440 | tf_op jit(solution)/shard_map/while/body/eval_jaxpr/ppermute | solution.py:13
  587.7 9.8 %collective-permute-start = (f32[128,512]{1,0:T(8,128)S(1)}, f32[128,512]{1,0:T(8,128)S(1)}, u32[]{:S(2)}, u32[]{:S(2)}) collective-permute-start(f32[128,512]{1,0:T(8,128)S(1)} %multiply_add_fusion.7), channel_id=1, source_target_pairs={{4,0},{8,4},{12,8},{16,12},{20,16},{24,20},{28,24},{32,28},{36,32}... | collective-permute-start | bytes 786440 | tf_op jit(solution)/shard_map/while/body/eval_jaxpr/ppermute | solution.py:13
  597.6 9.8 %collective-permute-start = (f32[128,512]{1,0:T(8,128)S(1)}, f32[128,512]{1,0:T(8,128)S(1)}, u32[]{:S(2)}, u32[]{:S(2)}) collective-permute-start(f32[128,512]{1,0:T(8,128)S(1)} %multiply_add_fusion.7), channel_id=1, source_target_pairs={{4,0},{8,4},{12,8},{16,12},{20,16},{24,20},{28,24},{32,28},{36,32}... | collective-permute-start | bytes 786440 | tf_op jit(solution)/shard_map/while/body/eval_jaxpr/ppermute | solution.py:13
  607.5 9.8 %collective-permute-start = (f32[128,512]{1,0:T(8,128)S(1)}, f32[128,512]{1,0:T(8,128)S(1)}, u32[]{:S(2)}, u32[]{:S(2)}) collective-permute-start(f32[128,512]{1,0:T(8,128)S(1)} %multiply_add_fusion.7), channel_id=1, source_target_pairs={{4,0},{8,4},{12,8},{16,12},{20,16},{24,20},{28,24},{32,28},{36,32}... | collective-permute-start | bytes 786440 | tf_op jit(solution)/shard_map/while/body/eval_jaxpr/ppermute | solution.py:13
  617.4 9.8 %collective-permute-start = (f32[128,512]{1,0:T(8,128)S(1)}, f32[128,512]{1,0:T(8,128)S(1)}, u32[]{:S(2)}, u32[]{:S(2)}) collective-permute-start(f32[128,512]{1,0:T(8,128)S(1)} %multiply_add_fusion.7), channel_id=1, source_target_pairs={{4,0},{8,4},{12,8},{16,12},{20,16},{24,20},{28,24},{32,28},{36,32}... | collective-permute-start | bytes 786440 | tf_op jit(solution)/shard_map/while/body/eval_jaxpr/ppermute | solution.py:13
  627.3 9.8 %collective-permute-start = (f32[128,512]{1,0:T(8,128)S(1)}, f32[128,512]{1,0:T(8,128)S(1)}, u32[]{:S(2)}, u32[]{:S(2)}) collective-permute-start(f32[128,512]{1,0:T(8,128)S(1)} %multiply_add_fusion.7), channel_id=1, source_target_pairs={{4,0},{8,4},{12,8},{16,12},{20,16},{24,20},{28,24},{32,28},{36,32}... | collective-permute-start | bytes 786440 | tf_op jit(solution)/shard_map/while/body/eval_jaxpr/ppermute | solution.py:13
  637.2 9.8 %collective-permute-start = (f32[128,512]{1,0:T(8,128)S(1)}, f32[128,512]{1,0:T(8,128)S(1)}, u32[]{:S(2)}, u32[]{:S(2)}) collective-permute-start(f32[128,512]{1,0:T(8,128)S(1)} %multiply_add_fusion.7), channel_id=1, source_target_pairs={{4,0},{8,4},{12,8},{16,12},{20,16},{24,20},{28,24},{32,28},{36,32}... | collective-permute-start | bytes 786440 | tf_op jit(solution)/shard_map/while/body/eval_jaxpr/ppermute | solution.py:13
  647.1 9.8 %collective-permute-start = (f32[128,512]{1,0:T(8,128)S(1)}, f32[128,512]{1,0:T(8,128)S(1)}, u32[]{:S(2)}, u32[]{:S(2)}) collective-permute-start(f32[128,512]{1,0:T(8,128)S(1)} %multiply_add_fusion.7), channel_id=1, source_target_pairs={{4,0},{8,4},{12,8},{16,12},{20,16},{24,20},{28,24},{32,28},{36,32}... | collective-permute-start | bytes 786440 | tf_op jit(solution)/shard_map/while/body/eval_jaxpr/ppermute | solution.py:13
  657.0 9.8 %collective-permute-start = (f32[128,512]{1,0:T(8,128)S(1)}, f32[128,512]{1,0:T(8,128)S(1)}, u32[]{:S(2)}, u32[]{:S(2)}) collective-permute-start(f32[128,512]{1,0:T(8,128)S(1)} %multiply_add_fusion.7), channel_id=1, source_target_pairs={{4,0},{8,4},{12,8},{16,12},{20,16},{24,20},{28,24},{32,28},{36,32}... | collective-permute-start | bytes 786440 | tf_op jit(solution)/shard_map/while/body/eval_jaxpr/ppermute | solution.py:13
  (25 other events, 725.1 us)
Sparse Core Ops, SparseCore 0:
  296.9 53.3 all-gather.1
  352.6 32.0 reduce-scatter.1
  671.7 134.1 all-reduce.5
where the time goes:
time: 820 us; the launch traced here: 818 us
  waiting for transfers between devices  525 us (64%)
  starting transfers between devices  230 us (28%)
  other arithmetic  24.4 us (3%)
  between operations  14.1 us (2%)
  matrix products  12.6 us (2%)
  local copies, waits for them, and re-layouts  9.91 us (1%)
    ppermute x62, waiting for transfers between devices, passed_along(): lax.ppermute(value, axis, [(source, source + steps) for source in range(f...  318 us
    ppermute x62, starting transfers between devices, passed_along(): lax.ppermute(value, axis, [(source, source + steps) for source in range(f...  230 us
    psum x1, waiting for transfers between devices, body(): grad_b, grad_c = lax.psum((grad_b_part, grad_c_part), 'tm')  134 us
    all_gather x1, waiting for transfers between devices, body(): lax.all_gather(states_bf, 'chan', axis=1, tiled=True)  49.7 us
    reduce_scatter x1, waiting for transfers between devices, body(): lax.psum_scatter(jnp.einsum('kup,fkus->pfs', kernel_c, cot_stack, preferr...  23.6 us
  transfers between devices with their start and end apart: 65, of which 65 were waited for; matrix products, arithmetic and copies ran while one was open for 2% of the time, Pallas kernels for 0%

commit v1 on v0

--- a/solution.py
+++ b/solution.py
@@ -85,7 +85,19 @@
     grad_b_part = jnp.einsum(
         "fps,fkcs->kpc", adjoint_bf, input_stack, preferred_element_type=jnp.float32
     )
-    shifted = stencil_stack(lax.all_gather(states_bf, "chan", axis=1, tiled=True), W, 1)
+    shifted = stencil_stack(
+        jnp.concatenate(
+            lax.all_to_all(
+                jnp.stack([states_bf] * lax.axis_size("chan"), axis=0),
+                axis_name="chan",
+                split_axis=0,
+                concat_axis=0,
+            ),
+            axis=1,
+        ),
+        W,
+        1,
+    )
     grad_c_part = jnp.einsum(
         "fus,fkps->kup", cotangent, shifted, preferred_element_type=jnp.float32
     )

time: 820 us -> 791 us (0.965)
  waiting for transfers between devices: 525 us -> 493 us
    all_gather x1 -> x0, waiting for transfers between devices: 49.7 us -> none  [body(): lax.all_gather(states_bf, 'chan', axis=1, tiled=True)]
    ppermute x62, waiting for transfers between devices: 318 us -> 350 us  [passed_along(): lax.ppermute(value, axis, [(source, source + steps) for source in range(f...]
    reduce_scatter x1, waiting for transfers between devices: 23.6 us -> 0.01 us  [body(): lax.psum_scatter(jnp.einsum('kup,fkus->pfs', kernel_c, cot_stack, preferr...]
    all_to_all x0 -> x1, waiting for transfers between devices: none -> 9.72 us  [body(): lax.all_to_all(jnp.stack([states_bf] * lax.axis_size('chan'), axis=0), ax...]
  transfers between devices with their start and end apart: 65 -> 65, of which waited for: 65 -> 64; matrix products, arithmetic and copies ran while one was open for 2% -> 2% of each run, Pallas kernels for 0% -> 0%
where the time goes in v1:
time: 791 us; the launch traced here: 788 us
  waiting for transfers between devices  493 us (62%)
  starting transfers between devices  234 us (30%)
  other arithmetic  22.6 us (3%)
  between operations  14.4 us (2%)
  matrix products  12.6 us (2%)
  local copies, waits for them, and re-layouts  11.1 us (1%)
    ppermute x62, waiting for transfers between devices, passed_along(): lax.ppermute(value, axis, [(source, source + steps) for source in range(f...  350 us
    ppermute x62, starting transfers between devices, passed_along(): lax.ppermute(value, axis, [(source, source + steps) for source in range(f...  229 us
    psum x1, waiting for transfers between devices, body(): grad_b, grad_c = lax.psum((grad_b_part, grad_c_part), 'tm')  133 us
  transfers between devices with their start and end apart: 65, of which 64 were waited for; matrix products, arithmetic and copies ran while one was open for 2% of the time, Pallas kernels for 0%

profile of v1, /device:TPU:1, one launch (start us, length us, event | category | flops | bytes accessed | tf_op | source)
XLA Modules:
  0.0 788.4 jit_solution(6736808904901830316)
XLA Ops:
  25.6 275.2 %while.51 = (s32[]{:T(128)}, f32[128,512]{1,0:T(8,128)S(1)}, f32[128]{0:T(128)S(1)}, f32[128,512]{1,0:T(8,128)S(1)}, s32[]{:T(128)}) while((s32[]{:T(128)}, f32[128,512]{1,0:T(8,128)S(1)}, f32[128]{0:T(128)S(1)}, f32[128,512]{1,0:T(8,128)S(1)}, s32[]{:T(128)}) %tuple.105), condition=%wide.region_12.13_spmd, body=%wide.region_11.12_spmd.sunk | while | flops 131074 | bytes 1835621 | solution.py:54
  152.4 6.5 collective-permute-start.1
  162.3 6.5 collective-permute-start.1
  172.2 6.5 collective-permute-start.1
  182.1 6.5 collective-permute-start.1
  192.0 6.5 collective-permute-start.1
  201.9 6.5 collective-permute-start.1
  211.8 6.5 collective-permute-start.1
  221.7 6.5 collective-permute-start.1
  231.6 6.5 collective-permute-start.1
  241.5 6.5 collective-permute-start.1
  251.4 6.5 collective-permute-start.1
  261.3 6.5 collective-permute-start.1
  271.2 6.5 collective-permute-start.1
  281.1 6.5 collective-permute-start.1
  291.0 6.5 collective-permute-start.1
  306.3 9.7 %all-to-all-done = bf16[4,2,128,512]{3,2,1,0:T(8,128)(2,1)S(1)} async-done(((bf16[4,2,128,512]{3,2,1,0:T(8,128)(2,1)}), bf16[4,2,128,512]{3,2,1,0:T(8,128)(2,1)S(1)}, u32[]{:S(2)}, u32[]{:S(2)}) %all-to-all-start) | async-done | bytes 1048608 | tf_op jit(solution)/shard_map/all_to_all | solution.py:90
  327.2 310.7 %while.50 = (s32[]{:T(128)}, f32[128,512]{1,0:T(8,128)S(1)}, f32[128]{0:T(128)S(1)}, f32[128,512]{1,0:T(8,128)S(1)}, s32[]{:T(128)}) while((s32[]{:T(128)}, f32[128,512]{1,0:T(8,128)S(1)}, f32[128]{0:T(128)S(1)}, f32[128,512]{1,0:T(8,128)S(1)}, s32[]{:T(128)}) %tuple.115), condition=%wide.region_6.7_spmd, body=%wide.region_5.6_spmd.sunk | while | flops 131074 | bytes 1835621 | solution.py:79
  329.3 10.0 %collective-permute-done = f32[128,512]{1,0:T(8,128)S(1)} collective-permute-done((f32[128,512]{1,0:T(8,128)S(1)}, f32[128,512]{1,0:T(8,128)S(1)}, u32[]{:S(2)}, u32[]{:S(2)}) %collective-permute-start) | collective-permute-done | bytes 262176 | tf_op jit(solution)/shard_map/while/body/eval_jaxpr/ppermute | solution.py:13
  341.3 6.3 collective-permute-done
  349.7 10.0 %collective-permute-done = f32[128,512]{1,0:T(8,128)S(1)} collective-permute-done((f32[128,512]{1,0:T(8,128)S(1)}, f32[128,512]{1,0:T(8,128)S(1)}, u32[]{:S(2)}, u32[]{:S(2)}) %collective-permute-start) | collective-permute-done | bytes 262176 | tf_op jit(solution)/shard_map/while/body/eval_jaxpr/ppermute | solution.py:13
  370.1 10.0 %collective-permute-done = f32[128,512]{1,0:T(8,128)S(1)} collective-permute-done((f32[128,512]{1,0:T(8,128)S(1)}, f32[128,512]{1,0:T(8,128)S(1)}, u32[]{:S(2)}, u32[]{:S(2)}) %collective-permute-start) | collective-permute-done | bytes 262176 | tf_op jit(solution)/shard_map/while/body/eval_jaxpr/ppermute | solution.py:13
  390.5 9.9 %collective-permute-done = f32[128,512]{1,0:T(8,128)S(1)} collective-permute-done((f32[128,512]{1,0:T(8,128)S(1)}, f32[128,512]{1,0:T(8,128)S(1)}, u32[]{:S(2)}, u32[]{:S(2)}) %collective-permute-start) | collective-permute-done | bytes 262176 | tf_op jit(solution)/shard_map/while/body/eval_jaxpr/ppermute | solution.py:13
  402.4 7.9 collective-permute-done
  412.3 7.9 collective-permute-done
  422.2 7.9 collective-permute-done
  432.1 7.9 collective-permute-done
  442.0 7.9 collective-permute-done
  451.9 7.9 collective-permute-done
  461.8 7.9 collective-permute-done
  471.7 7.9 collective-permute-done
  481.6 7.9 collective-permute-done
  491.5 7.9 collective-permute-done
  501.4 7.9 collective-permute-done
  511.3 7.9 collective-permute-done
  521.2 7.9 collective-permute-done
  531.1 7.9 collective-permute-done
  541.0 7.9 collective-permute-done
  550.9 7.9 collective-permute-done
  560.8 7.9 collective-permute-done
  570.7 7.9 collective-permute-done
  580.6 7.9 collective-permute-done
  590.5 7.9 collective-permute-done
  600.4 7.9 collective-permute-done
  610.3 7.9 collective-permute-done
  620.2 7.9 collective-permute-done
  630.0 7.9 collective-permute-done
  643.6 132.9 %all-reduce.6.cloned.1.call-done = (f32[9,128,256]{1,2,0:T(8,128)}, f32[9,64,512]{2,1,0:T(8,128)}) async-done(((f32[9,128,256]{1,2,0:T(8,128)}, f32[9,64,512]{2,1,0:T(8,128)}), (f32[9,128,256]{1,2,0:T(8,128)}, f32[9,64,512]{2,1,0:T(8,128)})) %all-reduce.6.cloned.1.call-update) | async-done | bytes 2359312 | tf_op jit(solution)/shard_map/psum | solution.py:104
  (234 shorter events, 300.4 us)
Async XLA Ops:
  7.2 317.3 %reduce-scatter.2.cloned.1.call-start = ((), (), s32[]{:S(2)}) async-start(), calls=%async_computation.2 | async-start | bytes 2621440 | tf_op jit(solution)/shard_map/reduce_scatter | solution.py:60
  143.0 9.3 %collective-permute-start.1 = (f32[128,512]{1,0:T(8,128)S(1)}, f32[128,512]{1,0:T(8,128)S(1)}, u32[]{:S(2)}, u32[]{:S(2)}) collective-permute-start(f32[128,512]{1,0:T(8,128)S(1)} %multiply_add_fusion.8), channel_id=1, source_target_pairs={{0,4},{4,8},{8,12},{12,16},{16,20},{20,24},{24,28},{28,32},{32,36}... | collective-permute-start | bytes 786440 | tf_op jit(solution)/shard_map/while/body/eval_jaxpr/ppermute | solution.py:13
  152.4 9.8 %collective-permute-start.1 = (f32[128,512]{1,0:T(8,128)S(1)}, f32[128,512]{1,0:T(8,128)S(1)}, u32[]{:S(2)}, u32[]{:S(2)}) collective-permute-start(f32[128,512]{1,0:T(8,128)S(1)} %multiply_add_fusion.8), channel_id=1, source_target_pairs={{0,4},{4,8},{8,12},{12,16},{16,20},{20,24},{24,28},{28,32},{32,36}... | collective-permute-start | bytes 786440 | tf_op jit(solution)/shard_map/while/body/eval_jaxpr/ppermute | solution.py:13
  162.3 9.8 %collective-permute-start.1 = (f32[128,512]{1,0:T(8,128)S(1)}, f32[128,512]{1,0:T(8,128)S(1)}, u32[]{:S(2)}, u32[]{:S(2)}) collective-permute-start(f32[128,512]{1,0:T(8,128)S(1)} %multiply_add_fusion.8), channel_id=1, source_target_pairs={{0,4},{4,8},{8,12},{12,16},{16,20},{20,24},{24,28},{28,32},{32,36}... | collective-permute-start | bytes 786440 | tf_op jit(solution)/shard_map/while/body/eval_jaxpr/ppermute | solution.py:13
  172.2 9.8 %collective-permute-start.1 = (f32[128,512]{1,0:T(8,128)S(1)}, f32[128,512]{1,0:T(8,128)S(1)}, u32[]{:S(2)}, u32[]{:S(2)}) collective-permute-start(f32[128,512]{1,0:T(8,128)S(1)} %multiply_add_fusion.8), channel_id=1, source_target_pairs={{0,4},{4,8},{8,12},{12,16},{16,20},{20,24},{24,28},{28,32},{32,36}... | collective-permute-start | bytes 786440 | tf_op jit(solution)/shard_map/while/body/eval_jaxpr/ppermute | solution.py:13
  182.1 9.8 %collective-permute-start.1 = (f32[128,512]{1,0:T(8,128)S(1)}, f32[128,512]{1,0:T(8,128)S(1)}, u32[]{:S(2)}, u32[]{:S(2)}) collective-permute-start(f32[128,512]{1,0:T(8,128)S(1)} %multiply_add_fusion.8), channel_id=1, source_target_pairs={{0,4},{4,8},{8,12},{12,16},{16,20},{20,24},{24,28},{28,32},{32,36}... | collective-permute-start | bytes 786440 | tf_op jit(solution)/shard_map/while/body/eval_jaxpr/ppermute | solution.py:13
  192.0 9.8 %collective-permute-start.1 = (f32[128,512]{1,0:T(8,128)S(1)}, f32[128,512]{1,0:T(8,128)S(1)}, u32[]{:S(2)}, u32[]{:S(2)}) collective-permute-start(f32[128,512]{1,0:T(8,128)S(1)} %multiply_add_fusion.8), channel_id=1, source_target_pairs={{0,4},{4,8},{8,12},{12,16},{16,20},{20,24},{24,28},{28,32},{32,36}... | collective-permute-start | bytes 786440 | tf_op jit(solution)/shard_map/while/body/eval_jaxpr/ppermute | solution.py:13
  201.9 9.8 %collective-permute-start.1 = (f32[128,512]{1,0:T(8,128)S(1)}, f32[128,512]{1,0:T(8,128)S(1)}, u32[]{:S(2)}, u32[]{:S(2)}) collective-permute-start(f32[128,512]{1,0:T(8,128)S(1)} %multiply_add_fusion.8), channel_id=1, source_target_pairs={{0,4},{4,8},{8,12},{12,16},{16,20},{20,24},{24,28},{28,32},{32,36}... | collective-permute-start | bytes 786440 | tf_op jit(solution)/shard_map/while/body/eval_jaxpr/ppermute | solution.py:13
  211.8 9.8 %collective-permute-start.1 = (f32[128,512]{1,0:T(8,128)S(1)}, f32[128,512]{1,0:T(8,128)S(1)}, u32[]{:S(2)}, u32[]{:S(2)}) collective-permute-start(f32[128,512]{1,0:T(8,128)S(1)} %multiply_add_fusion.8), channel_id=1, source_target_pairs={{0,4},{4,8},{8,12},{12,16},{16,20},{20,24},{24,28},{28,32},{32,36}... | collective-permute-start | bytes 786440 | tf_op jit(solution)/shard_map/while/body/eval_jaxpr/ppermute | solution.py:13
  221.7 9.8 %collective-permute-start.1 = (f32[128,512]{1,0:T(8,128)S(1)}, f32[128,512]{1,0:T(8,128)S(1)}, u32[]{:S(2)}, u32[]{:S(2)}) collective-permute-start(f32[128,512]{1,0:T(8,128)S(1)} %multiply_add_fusion.8), channel_id=1, source_target_pairs={{0,4},{4,8},{8,12},{12,16},{16,20},{20,24},{24,28},{28,32},{32,36}... | collective-permute-start | bytes 786440 | tf_op jit(solution)/shard_map/while/body/eval_jaxpr/ppermute | solution.py:13
  231.6 9.8 %collective-permute-start.1 = (f32[128,512]{1,0:T(8,128)S(1)}, f32[128,512]{1,0:T(8,128)S(1)}, u32[]{:S(2)}, u32[]{:S(2)}) collective-permute-start(f32[128,512]{1,0:T(8,128)S(1)} %multiply_add_fusion.8), channel_id=1, source_target_pairs={{0,4},{4,8},{8,12},{12,16},{16,20},{20,24},{24,28},{28,32},{32,36}... | collective-permute-start | bytes 786440 | tf_op jit(solution)/shard_map/while/body/eval_jaxpr/ppermute | solution.py:13
  241.5 9.8 %collective-permute-start.1 = (f32[128,512]{1,0:T(8,128)S(1)}, f32[128,512]{1,0:T(8,128)S(1)}, u32[]{:S(2)}, u32[]{:S(2)}) collective-permute-start(f32[128,512]{1,0:T(8,128)S(1)} %multiply_add_fusion.8), channel_id=1, source_target_pairs={{0,4},{4,8},{8,12},{12,16},{16,20},{20,24},{24,28},{28,32},{32,36}... | collective-permute-start | bytes 786440 | tf_op jit(solution)/shard_map/while/body/eval_jaxpr/ppermute | solution.py:13
  251.4 9.8 %collective-permute-start.1 = (f32[128,512]{1,0:T(8,128)S(1)}, f32[128,512]{1,0:T(8,128)S(1)}, u32[]{:S(2)}, u32[]{:S(2)}) collective-permute-start(f32[128,512]{1,0:T(8,128)S(1)} %multiply_add_fusion.8), channel_id=1, source_target_pairs={{0,4},{4,8},{8,12},{12,16},{16,20},{20,24},{24,28},{28,32},{32,36}... | collective-permute-start | bytes 786440 | tf_op jit(solution)/shard_map/while/body/eval_jaxpr/ppermute | solution.py:13
  261.3 9.8 %collective-permute-start.1 = (f32[128,512]{1,0:T(8,128)S(1)}, f32[128,512]{1,0:T(8,128)S(1)}, u32[]{:S(2)}, u32[]{:S(2)}) collective-permute-start(f32[128,512]{1,0:T(8,128)S(1)} %multiply_add_fusion.8), channel_id=1, source_target_pairs={{0,4},{4,8},{8,12},{12,16},{16,20},{20,24},{24,28},{28,32},{32,36}... | collective-permute-start | bytes 786440 | tf_op jit(solution)/shard_map/while/body/eval_jaxpr/ppermute | solution.py:13
  271.2 9.8 %collective-permute-start.1 = (f32[128,512]{1,0:T(8,128)S(1)}, f32[128,512]{1,0:T(8,128)S(1)}, u32[]{:S(2)}, u32[]{:S(2)}) collective-permute-start(f32[128,512]{1,0:T(8,128)S(1)} %multiply_add_fusion.8), channel_id=1, source_target_pairs={{0,4},{4,8},{8,12},{12,16},{16,20},{20,24},{24,28},{28,32},{32,36}... | collective-permute-start | bytes 786440 | tf_op jit(solution)/shard_map/while/body/eval_jaxpr/ppermute | solution.py:13
  281.1 9.8 %collective-permute-start.1 = (f32[128,512]{1,0:T(8,128)S(1)}, f32[128,512]{1,0:T(8,128)S(1)}, u32[]{:S(2)}, u32[]{:S(2)}) collective-permute-start(f32[128,512]{1,0:T(8,128)S(1)} %multiply_add_fusion.8), channel_id=1, source_target_pairs={{0,4},{4,8},{8,12},{12,16},{16,20},{20,24},{24,28},{28,32},{32,36}... | collective-permute-start | bytes 786440 | tf_op jit(solution)/shard_map/while/body/eval_jaxpr/ppermute | solution.py:13
  291.0 9.8 %collective-permute-start.1 = (f32[128,512]{1,0:T(8,128)S(1)}, f32[128,512]{1,0:T(8,128)S(1)}, u32[]{:S(2)}, u32[]{:S(2)}) collective-permute-start(f32[128,512]{1,0:T(8,128)S(1)} %multiply_add_fusion.8), channel_id=1, source_target_pairs={{0,4},{4,8},{8,12},{12,16},{16,20},{20,24},{24,28},{28,32},{32,36}... | collective-permute-start | bytes 786440 | tf_op jit(solution)/shard_map/while/body/eval_jaxpr/ppermute | solution.py:13
  302.0 14.1 %all-to-all-start = ((bf16[4,2,128,512]{3,2,1,0:T(8,128)(2,1)}), bf16[4,2,128,512]{3,2,1,0:T(8,128)(2,1)S(1)}, u32[]{:S(2)}, u32[]{:S(2)}) async-start(bf16[4,2,128,512]{3,2,1,0:T(8,128)(2,1)} %stack.115), calls=%async_computation.1 | async-start | bytes 2097152 | tf_op jit(solution)/shard_map/all_to_all | solution.py:90
  306.2 470.3 %all-reduce.6.cloned.1.call-start = ((), (), s32[]{:S(2)}) async-start(), calls=%async_computation.3 | async-start | bytes 4718592 | tf_op jit(solution)/shard_map/psum | solution.py:104
  327.3 12.0 %collective-permute-start = (f32[128,512]{1,0:T(8,128)S(1)}, f32[128,512]{1,0:T(8,128)S(1)}, u32[]{:S(2)}, u32[]{:S(2)}) collective-permute-start(f32[128,512]{1,0:T(8,128)S(1)} %multiply_add_fusion.7), channel_id=1, source_target_pairs={{4,0},{8,4},{12,8},{16,12},{20,16},{24,20},{28,24},{32,28},{36,32}... | collective-permute-start | bytes 786440 | tf_op jit(solution)/shard_map/while/body/eval_jaxpr/ppermute | solution.py:13
  339.4 8.2 %collective-permute-start = (f32[128,512]{1,0:T(8,128)S(1)}, f32[128,512]{1,0:T(8,128)S(1)}, u32[]{:S(2)}, u32[]{:S(2)}) collective-permute-start(f32[128,512]{1,0:T(8,128)S(1)} %multiply_add_fusion.7), channel_id=1, source_target_pairs={{4,0},{8,4},{12,8},{16,12},{20,16},{24,20},{28,24},{32,28},{36,32}... | collective-permute-start | bytes 786440 | tf_op jit(solution)/shard_map/while/body/eval_jaxpr/ppermute | solution.py:13
  347.7 12.0 %collective-permute-start = (f32[128,512]{1,0:T(8,128)S(1)}, f32[128,512]{1,0:T(8,128)S(1)}, u32[]{:S(2)}, u32[]{:S(2)}) collective-permute-start(f32[128,512]{1,0:T(8,128)S(1)} %multiply_add_fusion.7), channel_id=1, source_target_pairs={{4,0},{8,4},{12,8},{16,12},{20,16},{24,20},{28,24},{32,28},{36,32}... | collective-permute-start | bytes 786440 | tf_op jit(solution)/shard_map/while/body/eval_jaxpr/ppermute | solution.py:13
  368.2 12.0 %collective-permute-start = (f32[128,512]{1,0:T(8,128)S(1)}, f32[128,512]{1,0:T(8,128)S(1)}, u32[]{:S(2)}, u32[]{:S(2)}) collective-permute-start(f32[128,512]{1,0:T(8,128)S(1)} %multiply_add_fusion.7), channel_id=1, source_target_pairs={{4,0},{8,4},{12,8},{16,12},{20,16},{24,20},{28,24},{32,28},{36,32}... | collective-permute-start | bytes 786440 | tf_op jit(solution)/shard_map/while/body/eval_jaxpr/ppermute | solution.py:13
  388.6 11.9 %collective-permute-start = (f32[128,512]{1,0:T(8,128)S(1)}, f32[128,512]{1,0:T(8,128)S(1)}, u32[]{:S(2)}, u32[]{:S(2)}) collective-permute-start(f32[128,512]{1,0:T(8,128)S(1)} %multiply_add_fusion.7), channel_id=1, source_target_pairs={{4,0},{8,4},{12,8},{16,12},{20,16},{24,20},{28,24},{32,28},{36,32}... | collective-permute-start | bytes 786440 | tf_op jit(solution)/shard_map/while/body/eval_jaxpr/ppermute | solution.py:13
  400.5 9.8 %collective-permute-start = (f32[128,512]{1,0:T(8,128)S(1)}, f32[128,512]{1,0:T(8,128)S(1)}, u32[]{:S(2)}, u32[]{:S(2)}) collective-permute-start(f32[128,512]{1,0:T(8,128)S(1)} %multiply_add_fusion.7), channel_id=1, source_target_pairs={{4,0},{8,4},{12,8},{16,12},{20,16},{24,20},{28,24},{32,28},{36,32}... | collective-permute-start | bytes 786440 | tf_op jit(solution)/shard_map/while/body/eval_jaxpr/ppermute | solution.py:13
  410.4 9.8 %collective-permute-start = (f32[128,512]{1,0:T(8,128)S(1)}, f32[128,512]{1,0:T(8,128)S(1)}, u32[]{:S(2)}, u32[]{:S(2)}) collective-permute-start(f32[128,512]{1,0:T(8,128)S(1)} %multiply_add_fusion.7), channel_id=1, source_target_pairs={{4,0},{8,4},{12,8},{16,12},{20,16},{24,20},{28,24},{32,28},{36,32}... | collective-permute-start | bytes 786440 | tf_op jit(solution)/shard_map/while/body/eval_jaxpr/ppermute | solution.py:13
  420.3 9.8 %collective-permute-start = (f32[128,512]{1,0:T(8,128)S(1)}, f32[128,512]{1,0:T(8,128)S(1)}, u32[]{:S(2)}, u32[]{:S(2)}) collective-permute-start(f32[128,512]{1,0:T(8,128)S(1)} %multiply_add_fusion.7), channel_id=1, source_target_pairs={{4,0},{8,4},{12,8},{16,12},{20,16},{24,20},{28,24},{32,28},{36,32}... | collective-permute-start | bytes 786440 | tf_op jit(solution)/shard_map/while/body/eval_jaxpr/ppermute | solution.py:13
  430.2 9.8 %collective-permute-start = (f32[128,512]{1,0:T(8,128)S(1)}, f32[128,512]{1,0:T(8,128)S(1)}, u32[]{:S(2)}, u32[]{:S(2)}) collective-permute-start(f32[128,512]{1,0:T(8,128)S(1)} %multiply_add_fusion.7), channel_id=1, source_target_pairs={{4,0},{8,4},{12,8},{16,12},{20,16},{24,20},{28,24},{32,28},{36,32}... | collective-permute-start | bytes 786440 | tf_op jit(solution)/shard_map/while/body/eval_jaxpr/ppermute | solution.py:13
  440.1 9.8 %collective-permute-start = (f32[128,512]{1,0:T(8,128)S(1)}, f32[128,512]{1,0:T(8,128)S(1)}, u32[]{:S(2)}, u32[]{:S(2)}) collective-permute-start(f32[128,512]{1,0:T(8,128)S(1)} %multiply_add_fusion.7), channel_id=1, source_target_pairs={{4,0},{8,4},{12,8},{16,12},{20,16},{24,20},{28,24},{32,28},{36,32}... | collective-permute-start | bytes 786440 | tf_op jit(solution)/shard_map/while/body/eval_jaxpr/ppermute | solution.py:13
  450.0 9.8 %collective-permute-start = (f32[128,512]{1,0:T(8,128)S(1)}, f32[128,512]{1,0:T(8,128)S(1)}, u32[]{:S(2)}, u32[]{:S(2)}) collective-permute-start(f32[128,512]{1,0:T(8,128)S(1)} %multiply_add_fusion.7), channel_id=1, source_target_pairs={{4,0},{8,4},{12,8},{16,12},{20,16},{24,20},{28,24},{32,28},{36,32}... | collective-permute-start | bytes 786440 | tf_op jit(solution)/shard_map/while/body/eval_jaxpr/ppermute | solution.py:13
  459.9 9.8 %collective-permute-start = (f32[128,512]{1,0:T(8,128)S(1)}, f32[128,512]{1,0:T(8,128)S(1)}, u32[]{:S(2)}, u32[]{:S(2)}) collective-permute-start(f32[128,512]{1,0:T(8,128)S(1)} %multiply_add_fusion.7), channel_id=1, source_target_pairs={{4,0},{8,4},{12,8},{16,12},{20,16},{24,20},{28,24},{32,28},{36,32}... | collective-permute-start | bytes 786440 | tf_op jit(solution)/shard_map/while/body/eval_jaxpr/ppermute | solution.py:13
  469.8 9.8 %collective-permute-start = (f32[128,512]{1,0:T(8,128)S(1)}, f32[128,512]{1,0:T(8,128)S(1)}, u32[]{:S(2)}, u32[]{:S(2)}) collective-permute-start(f32[128,512]{1,0:T(8,128)S(1)} %multiply_add_fusion.7), channel_id=1, source_target_pairs={{4,0},{8,4},{12,8},{16,12},{20,16},{24,20},{28,24},{32,28},{36,32}... | collective-permute-start | bytes 786440 | tf_op jit(solution)/shard_map/while/body/eval_jaxpr/ppermute | solution.py:13
  479.7 9.8 %collective-permute-start = (f32[128,512]{1,0:T(8,128)S(1)}, f32[128,512]{1,0:T(8,128)S(1)}, u32[]{:S(2)}, u32[]{:S(2)}) collective-permute-start(f32[128,512]{1,0:T(8,128)S(1)} %multiply_add_fusion.7), channel_id=1, source_target_pairs={{4,0},{8,4},{12,8},{16,12},{20,16},{24,20},{28,24},{32,28},{36,32}... | collective-permute-start | bytes 786440 | tf_op jit(solution)/shard_map/while/body/eval_jaxpr/ppermute | solution.py:13
  489.6 9.8 %collective-permute-start = (f32[128,512]{1,0:T(8,128)S(1)}, f32[128,512]{1,0:T(8,128)S(1)}, u32[]{:S(2)}, u32[]{:S(2)}) collective-permute-start(f32[128,512]{1,0:T(8,128)S(1)} %multiply_add_fusion.7), channel_id=1, source_target_pairs={{4,0},{8,4},{12,8},{16,12},{20,16},{24,20},{28,24},{32,28},{36,32}... | collective-permute-start | bytes 786440 | tf_op jit(solution)/shard_map/while/body/eval_jaxpr/ppermute | solution.py:13
  499.5 9.8 %collective-permute-start = (f32[128,512]{1,0:T(8,128)S(1)}, f32[128,512]{1,0:T(8,128)S(1)}, u32[]{:S(2)}, u32[]{:S(2)}) collective-permute-start(f32[128,512]{1,0:T(8,128)S(1)} %multiply_add_fusion.7), channel_id=1, source_target_pairs={{4,0},{8,4},{12,8},{16,12},{20,16},{24,20},{28,24},{32,28},{36,32}... | collective-permute-start | bytes 786440 | tf_op jit(solution)/shard_map/while/body/eval_jaxpr/ppermute | solution.py:13
  509.4 9.8 %collective-permute-start = (f32[128,512]{1,0:T(8,128)S(1)}, f32[128,512]{1,0:T(8,128)S(1)}, u32[]{:S(2)}, u32[]{:S(2)}) collective-permute-start(f32[128,512]{1,0:T(8,128)S(1)} %multiply_add_fusion.7), channel_id=1, source_target_pairs={{4,0},{8,4},{12,8},{16,12},{20,16},{24,20},{28,24},{32,28},{36,32}... | collective-permute-start | bytes 786440 | tf_op jit(solution)/shard_map/while/body/eval_jaxpr/ppermute | solution.py:13
  519.3 9.8 %collective-permute-start = (f32[128,512]{1,0:T(8,128)S(1)}, f32[128,512]{1,0:T(8,128)S(1)}, u32[]{:S(2)}, u32[]{:S(2)}) collective-permute-start(f32[128,512]{1,0:T(8,128)S(1)} %multiply_add_fusion.7), channel_id=1, source_target_pairs={{4,0},{8,4},{12,8},{16,12},{20,16},{24,20},{28,24},{32,28},{36,32}... | collective-permute-start | bytes 786440 | tf_op jit(solution)/shard_map/while/body/eval_jaxpr/ppermute | solution.py:13
  529.2 9.8 %collective-permute-start = (f32[128,512]{1,0:T(8,128)S(1)}, f32[128,512]{1,0:T(8,128)S(1)}, u32[]{:S(2)}, u32[]{:S(2)}) collective-permute-start(f32[128,512]{1,0:T(8,128)S(1)} %multiply_add_fusion.7), channel_id=1, source_target_pairs={{4,0},{8,4},{12,8},{16,12},{20,16},{24,20},{28,24},{32,28},{36,32}... | collective-permute-start | bytes 786440 | tf_op jit(solution)/shard_map/while/body/eval_jaxpr/ppermute | solution.py:13
  539.1 9.8 %collective-permute-start = (f32[128,512]{1,0:T(8,128)S(1)}, f32[128,512]{1,0:T(8,128)S(1)}, u32[]{:S(2)}, u32[]{:S(2)}) collective-permute-start(f32[128,512]{1,0:T(8,128)S(1)} %multiply_add_fusion.7), channel_id=1, source_target_pairs={{4,0},{8,4},{12,8},{16,12},{20,16},{24,20},{28,24},{32,28},{36,32}... | collective-permute-start | bytes 786440 | tf_op jit(solution)/shard_map/while/body/eval_jaxpr/ppermute | solution.py:13
  549.0 9.8 %collective-permute-start = (f32[128,512]{1,0:T(8,128)S(1)}, f32[128,512]{1,0:T(8,128)S(1)}, u32[]{:S(2)}, u32[]{:S(2)}) collective-permute-start(f32[128,512]{1,0:T(8,128)S(1)} %multiply_add_fusion.7), channel_id=1, source_target_pairs={{4,0},{8,4},{12,8},{16,12},{20,16},{24,20},{28,24},{32,28},{36,32}... | collective-permute-start | bytes 786440 | tf_op jit(solution)/shard_map/while/body/eval_jaxpr/ppermute | solution.py:13
  558.8 9.8 %collective-permute-start = (f32[128,512]{1,0:T(8,128)S(1)}, f32[128,512]{1,0:T(8,128)S(1)}, u32[]{:S(2)}, u32[]{:S(2)}) collective-permute-start(f32[128,512]{1,0:T(8,128)S(1)} %multiply_add_fusion.7), channel_id=1, source_target_pairs={{4,0},{8,4},{12,8},{16,12},{20,16},{24,20},{28,24},{32,28},{36,32}... | collective-permute-start | bytes 786440 | tf_op jit(solution)/shard_map/while/body/eval_jaxpr/ppermute | solution.py:13
  568.7 9.8 %collective-permute-start = (f32[128,512]{1,0:T(8,128)S(1)}, f32[128,512]{1,0:T(8,128)S(1)}, u32[]{:S(2)}, u32[]{:S(2)}) collective-permute-start(f32[128,512]{1,0:T(8,128)S(1)} %multiply_add_fusion.7), channel_id=1, source_target_pairs={{4,0},{8,4},{12,8},{16,12},{20,16},{24,20},{28,24},{32,28},{36,32}... | collective-permute-start | bytes 786440 | tf_op jit(solution)/shard_map/while/body/eval_jaxpr/ppermute | solution.py:13
  578.6 9.8 %collective-permute-start = (f32[128,512]{1,0:T(8,128)S(1)}, f32[128,512]{1,0:T(8,128)S(1)}, u32[]{:S(2)}, u32[]{:S(2)}) collective-permute-start(f32[128,512]{1,0:T(8,128)S(1)} %multiply_add_fusion.7), channel_id=1, source_target_pairs={{4,0},{8,4},{12,8},{16,12},{20,16},{24,20},{28,24},{32,28},{36,32}... | collective-permute-start | bytes 786440 | tf_op jit(solution)/shard_map/while/body/eval_jaxpr/ppermute | solution.py:13
  588.5 9.8 %collective-permute-start = (f32[128,512]{1,0:T(8,128)S(1)}, f32[128,512]{1,0:T(8,128)S(1)}, u32[]{:S(2)}, u32[]{:S(2)}) collective-permute-start(f32[128,512]{1,0:T(8,128)S(1)} %multiply_add_fusion.7), channel_id=1, source_target_pairs={{4,0},{8,4},{12,8},{16,12},{20,16},{24,20},{28,24},{32,28},{36,32}... | collective-permute-start | bytes 786440 | tf_op jit(solution)/shard_map/while/body/eval_jaxpr/ppermute | solution.py:13
  598.4 9.8 %collective-permute-start = (f32[128,512]{1,0:T(8,128)S(1)}, f32[128,512]{1,0:T(8,128)S(1)}, u32[]{:S(2)}, u32[]{:S(2)}) collective-permute-start(f32[128,512]{1,0:T(8,128)S(1)} %multiply_add_fusion.7), channel_id=1, source_target_pairs={{4,0},{8,4},{12,8},{16,12},{20,16},{24,20},{28,24},{32,28},{36,32}... | collective-permute-start | bytes 786440 | tf_op jit(solution)/shard_map/while/body/eval_jaxpr/ppermute | solution.py:13
  608.3 9.8 %collective-permute-start = (f32[128,512]{1,0:T(8,128)S(1)}, f32[128,512]{1,0:T(8,128)S(1)}, u32[]{:S(2)}, u32[]{:S(2)}) collective-permute-start(f32[128,512]{1,0:T(8,128)S(1)} %multiply_add_fusion.7), channel_id=1, source_target_pairs={{4,0},{8,4},{12,8},{16,12},{20,16},{24,20},{28,24},{32,28},{36,32}... | collective-permute-start | bytes 786440 | tf_op jit(solution)/shard_map/while/body/eval_jaxpr/ppermute | solution.py:13
  618.2 9.8 %collective-permute-start = (f32[128,512]{1,0:T(8,128)S(1)}, f32[128,512]{1,0:T(8,128)S(1)}, u32[]{:S(2)}, u32[]{:S(2)}) collective-permute-start(f32[128,512]{1,0:T(8,128)S(1)} %multiply_add_fusion.7), channel_id=1, source_target_pairs={{4,0},{8,4},{12,8},{16,12},{20,16},{24,20},{28,24},{32,28},{36,32}... | collective-permute-start | bytes 786440 | tf_op jit(solution)/shard_map/while/body/eval_jaxpr/ppermute | solution.py:13
  628.1 9.8 %collective-permute-start = (f32[128,512]{1,0:T(8,128)S(1)}, f32[128,512]{1,0:T(8,128)S(1)}, u32[]{:S(2)}, u32[]{:S(2)}) collective-permute-start(f32[128,512]{1,0:T(8,128)S(1)} %multiply_add_fusion.7), channel_id=1, source_target_pairs={{4,0},{8,4},{12,8},{16,12},{20,16},{24,20},{28,24},{32,28},{36,32}... | collective-permute-start | bytes 786440 | tf_op jit(solution)/shard_map/while/body/eval_jaxpr/ppermute | solution.py:13
  (24 other events, 436.0 us)
Sparse Core Ops, SparseCore 0:
  19.0 32.8 reduce-scatter.1
  642.9 133.5 all-reduce.5
